TPU v7x, 128 devices: a whole 4x4x4 slice. The times are simulated.
128 devices in a mesh: region: 64 (over z, y, x), chan: 2 (over core).
Axes of the slice: x: 4, y: 4, z: 4, core: 2. Of those that a mesh axis runs over, the one named last changes fastest.
Arguments:
- features: bfloat16 [384, 196608], P('chan', 'region'), may hold values from -6 to 6
- gain: float32 [384], P('chan'), may hold values from 0.1 to 1.9
- bias: float32 [384], P('chan'), may hold values from -3 to 3
- live: int32 [64], P('region'), may hold values from 1024 to 3072, as said below
- neighbors: int32 [27, 196608], P(None, 'region'), may hold values from -1 to 196607, as said below
- weights: bfloat16 [27, 384, 384], P(None, 'chan'), may hold values from -0.0625 to 0.0625
- grad_out: bfloat16 [384, 196608], P('chan', 'region'), may hold values from -0.059814453 to 0.059814453
Outputs:
- conv_out: bfloat16 [384, 196608], P('chan', 'region')
- kernel_grad: float32 [27, 384, 384], P(None, 'chan')
Inputs may be any that keep to these rules, and one draw needn't show every extreme that they name: One region has all 3072 slots counted live. `neighbors`: an entry [k, i] is -1 or the index of a live site at most 256 away from i; every entry of a site that is not live is -1.
All inputs are finite; a program needn't handle non-finite values.
Results may differ from a plain program's by a relative error of at most 0.0049.
Values may be sent and summed in bfloat16 or wider, within the bound.
No kernel may reach another device: no remote copies, remote signals or barrier semaphores. Data moves between devices by JAX's collectives and lax.ppermute only.
A program may use at most 128 MiB of HBM per device.

v0:
```python
import jax
import jax.numpy as jnp
import numpy as np
from jax import lax
from jax.sharding import Mesh
from jax.sharding import PartitionSpec as P

SUB = ("z", "y", "x")


def region_sum(x):
    for axis in reversed(SUB):
        x = lax.psum(x, axis)
    return x


def padded(x, width):
    count = lax.axis_size(SUB)
    length = x.shape[0]
    up = [(i, (i + 1) % count) for i in range(count - 1)]
    down = [(j, i) for i, j in up]
    last = lax.slice_in_dim(x, length - width, length, axis=0)
    first = lax.slice_in_dim(x, 0, width, axis=0)
    before = lax.ppermute(last, SUB, up)
    after = lax.ppermute(first, SUB, down)
    return jnp.concatenate([before, x, after], axis=0)


def per_device(features, gain, bias, live, neighbors, weights, grad_out):
    channels, columns = features.shape
    border = columns // 12
    region_idx = lax.axis_index(SUB)
    column = jnp.arange(columns, dtype=jnp.int32)
    live_limit = live[0] - border
    live_mask = ((column < live_limit) | (column >= columns - border)).astype(jnp.float32)
    values = features.astype(jnp.float32)
    masked = values * live_mask[None, :]
    live_rows = jnp.sum(live_mask)
    totals, live_total = region_sum((jnp.sum(masked, axis=1), live_rows))
    average = totals / live_total
    centered = (values - average[:, None]) * live_mask[None, :]
    variance = region_sum(jnp.sum(centered * centered, axis=1)) / live_total
    factor = gain * lax.rsqrt(variance + 1e-05)
    normed = (
        jnp.maximum((values - average[:, None]) * factor[:, None] + bias[:, None], 0.0)
        * live_mask[None, :]
    )
    site_rows = jnp.transpose(normed).astype(jnp.bfloat16)
    own_chans = lax.all_gather(site_rows, "chan", axis=1, tiled=True)
    gathered = padded(own_chans, border)
    anchor = region_idx * columns - border
    extent = columns + 2 * border

    def offset_step(running, operand):
        kernel, targets = operand
        position = jnp.where(targets < 0, extent, targets - anchor)
        picked = jnp.take(gathered, position, axis=0, mode="fill", fill_value=0)
        running = running + lax.dot_general(
            kernel, picked, (((1,), (1,)), ((), ())), preferred_element_type=jnp.float32
        )
        grad_piece = jnp.dot(grad_out, picked, preferred_element_type=jnp.float32)
        return (running, grad_piece)

    start = jnp.zeros((weights.shape[1], columns), jnp.float32)
    conv_sum, grad_parts = lax.scan(offset_step, start, (weights, neighbors))
    kernel_grad = region_sum(grad_parts)
    return (conv_sum.astype(jnp.bfloat16), kernel_grad)


def sub_mesh(mesh):
    devices = np.asarray(mesh.devices)
    count = devices.shape[0]
    first = devices[:, 0]
    try:
        sizes = [len({d.coords[a] for d in first}) for a in (2, 1, 0)]
    except (AttributeError, IndexError, TypeError):
        sizes = [count, 1, 1]
    if int(np.prod(sizes)) != count:
        sizes = [count, 1, 1]
    return Mesh(devices.reshape(*sizes, devices.shape[1]), SUB + ("chan",))


def solution(mesh):
    sites = ("chan", SUB)
    return jax.shard_map(
        per_device,
        mesh=sub_mesh(mesh),
        in_specs=(
            P(*sites),
            P("chan"),
            P("chan"),
            P(SUB),
            P(None, SUB),
            P(None, "chan", None),
            P(*sites),
        ),
        out_specs=(P(*sites), P(None, "chan", None)),
        check_vma=False,
    )
```

profile of v0, /device:TPU:1, one launch (start us, length us, event | category | flops | bytes accessed | tf_op | source)
XLA Modules:
  0.0 1149.2 jit_solution(16765144622355839185)
XLA Ops:
  10.2 9.9 all-reduce
  20.1 9.6 all-reduce.1
  29.7 10.4 all-reduce.2
  42.5 6.0 psum.90
  48.5 6.2 psum.91
  54.7 6.0 psum.92
  63.2 23.1 %all-gather.2.cloned.1.call-done = bf16[3072,384]{0,1:T(8,128)(2,1)} async-done(((bf16[3072,192]{0,1:T(8,128)(2,1)}), bf16[3072,384]{0,1:T(8,128)(2,1)}) %all-gather.2.cloned.1.call-update) | async-done | bytes 2359312 | tf_op jit(solution)/shard_map/all_gather | solution.py:49
  105.2 559.5 %while.13 = (s32[]{:T(128)}, f32[192,3072]{1,0:T(8,128)}, f32[27,192,384]{2,1,0:T(8,128)}, bf16[27,192,384]{2,1,0:T(8,128)(2,1)}, s32[27,3072]{1,0:T(8,128)}, /*...) while((s32[]{:T(128)}, f32[192,3072]{1,0:T(8,128)}, ...), condition=%wide.region_13.14_spmd.clone, body=%wide.region_12.13_spmd.clone.sunk | while | flops 909548544 | bytes 30030000 | solution.py:65
  106.2 13.0 %gather_fusion = bf16[3072,384]{1,0:T(8,128)(2,1)} fusion(bf16[3584,384]{1,0:T(8,128)(2,1)S(1)} %get-tuple-element.187, s32[3072]{0:T(1024)S(1)} %broadcast_clamp_fusion.2), kind=kCustom, calls=%fused_computation.clone.clone.1 | custom fusion | bytes 4730880 | tf_op jit(solution)/shard_map/while/body/eval_jaxpr/jit(_take)/gather | solution.py:57
  126.2 13.0 %gather_fusion = bf16[3072,384]{1,0:T(8,128)(2,1)} fusion(bf16[3584,384]{1,0:T(8,128)(2,1)S(1)} %get-tuple-element.187, s32[3072]{0:T(1024)S(1)} %broadcast_clamp_fusion.2), kind=kCustom, calls=%fused_computation.clone.clone.1 | custom fusion | bytes 4730880 | tf_op jit(solution)/shard_map/while/body/eval_jaxpr/jit(_take)/gather | solution.py:57
  139.3 5.1 convolution_add_fusion.2
  147.0 13.0 %gather_fusion = bf16[3072,384]{1,0:T(8,128)(2,1)} fusion(bf16[3584,384]{1,0:T(8,128)(2,1)S(1)} %get-tuple-element.187, s32[3072]{0:T(1024)S(1)} %broadcast_clamp_fusion.2), kind=kCustom, calls=%fused_computation.clone.clone.1 | custom fusion | bytes 4730880 | tf_op jit(solution)/shard_map/while/body/eval_jaxpr/jit(_take)/gather | solution.py:57
  160.1 5.1 convolution_add_fusion.2
  167.7 13.0 %gather_fusion = bf16[3072,384]{1,0:T(8,128)(2,1)} fusion(bf16[3584,384]{1,0:T(8,128)(2,1)S(1)} %get-tuple-element.187, s32[3072]{0:T(1024)S(1)} %broadcast_clamp_fusion.2), kind=kCustom, calls=%fused_computation.clone.clone.1 | custom fusion | bytes 4730880 | tf_op jit(solution)/shard_map/while/body/eval_jaxpr/jit(_take)/gather | solution.py:57
  180.8 5.1 convolution_add_fusion.2
  188.5 13.0 %gather_fusion = bf16[3072,384]{1,0:T(8,128)(2,1)} fusion(bf16[3584,384]{1,0:T(8,128)(2,1)S(1)} %get-tuple-element.187, s32[3072]{0:T(1024)S(1)} %broadcast_clamp_fusion.2), kind=kCustom, calls=%fused_computation.clone.clone.1 | custom fusion | bytes 4730880 | tf_op jit(solution)/shard_map/while/body/eval_jaxpr/jit(_take)/gather | solution.py:57
  201.6 5.1 convolution_add_fusion.2
  209.2 13.0 %gather_fusion = bf16[3072,384]{1,0:T(8,128)(2,1)} fusion(bf16[3584,384]{1,0:T(8,128)(2,1)S(1)} %get-tuple-element.187, s32[3072]{0:T(1024)S(1)} %broadcast_clamp_fusion.2), kind=kCustom, calls=%fused_computation.clone.clone.1 | custom fusion | bytes 4730880 | tf_op jit(solution)/shard_map/while/body/eval_jaxpr/jit(_take)/gather | solution.py:57
  222.3 5.1 convolution_add_fusion.2
  230.0 13.0 %gather_fusion = bf16[3072,384]{1,0:T(8,128)(2,1)} fusion(bf16[3584,384]{1,0:T(8,128)(2,1)S(1)} %get-tuple-element.187, s32[3072]{0:T(1024)S(1)} %broadcast_clamp_fusion.2), kind=kCustom, calls=%fused_computation.clone.clone.1 | custom fusion | bytes 4730880 | tf_op jit(solution)/shard_map/while/body/eval_jaxpr/jit(_take)/gather | solution.py:57
  243.1 5.1 convolution_add_fusion.2
  250.7 13.0 %gather_fusion = bf16[3072,384]{1,0:T(8,128)(2,1)} fusion(bf16[3584,384]{1,0:T(8,128)(2,1)S(1)} %get-tuple-element.187, s32[3072]{0:T(1024)S(1)} %broadcast_clamp_fusion.2), kind=kCustom, calls=%fused_computation.clone.clone.1 | custom fusion | bytes 4730880 | tf_op jit(solution)/shard_map/while/body/eval_jaxpr/jit(_take)/gather | solution.py:57
  263.8 5.1 convolution_add_fusion.2
  271.5 13.0 %gather_fusion = bf16[3072,384]{1,0:T(8,128)(2,1)} fusion(bf16[3584,384]{1,0:T(8,128)(2,1)S(1)} %get-tuple-element.187, s32[3072]{0:T(1024)S(1)} %broadcast_clamp_fusion.2), kind=kCustom, calls=%fused_computation.clone.clone.1 | custom fusion | bytes 4730880 | tf_op jit(solution)/shard_map/while/body/eval_jaxpr/jit(_take)/gather | solution.py:57
  284.6 5.1 convolution_add_fusion.2
  292.2 13.0 %gather_fusion = bf16[3072,384]{1,0:T(8,128)(2,1)} fusion(bf16[3584,384]{1,0:T(8,128)(2,1)S(1)} %get-tuple-element.187, s32[3072]{0:T(1024)S(1)} %broadcast_clamp_fusion.2), kind=kCustom, calls=%fused_computation.clone.clone.1 | custom fusion | bytes 4730880 | tf_op jit(solution)/shard_map/while/body/eval_jaxpr/jit(_take)/gather | solution.py:57
  305.3 5.1 convolution_add_fusion.2
  313.0 13.0 %gather_fusion = bf16[3072,384]{1,0:T(8,128)(2,1)} fusion(bf16[3584,384]{1,0:T(8,128)(2,1)S(1)} %get-tuple-element.187, s32[3072]{0:T(1024)S(1)} %broadcast_clamp_fusion.2), kind=kCustom, calls=%fused_computation.clone.clone.1 | custom fusion | bytes 4730880 | tf_op jit(solution)/shard_map/while/body/eval_jaxpr/jit(_take)/gather | solution.py:57
  326.1 5.1 convolution_add_fusion.2
  333.7 13.0 %gather_fusion = bf16[3072,384]{1,0:T(8,128)(2,1)} fusion(bf16[3584,384]{1,0:T(8,128)(2,1)S(1)} %get-tuple-element.187, s32[3072]{0:T(1024)S(1)} %broadcast_clamp_fusion.2), kind=kCustom, calls=%fused_computation.clone.clone.1 | custom fusion | bytes 4730880 | tf_op jit(solution)/shard_map/while/body/eval_jaxpr/jit(_take)/gather | solution.py:57
  346.8 5.1 convolution_add_fusion.2
  354.5 13.0 %gather_fusion = bf16[3072,384]{1,0:T(8,128)(2,1)} fusion(bf16[3584,384]{1,0:T(8,128)(2,1)S(1)} %get-tuple-element.187, s32[3072]{0:T(1024)S(1)} %broadcast_clamp_fusion.2), kind=kCustom, calls=%fused_computation.clone.clone.1 | custom fusion | bytes 4730880 | tf_op jit(solution)/shard_map/while/body/eval_jaxpr/jit(_take)/gather | solution.py:57
  367.6 5.1 convolution_add_fusion.2
  375.2 13.0 %gather_fusion = bf16[3072,384]{1,0:T(8,128)(2,1)} fusion(bf16[3584,384]{1,0:T(8,128)(2,1)S(1)} %get-tuple-element.187, s32[3072]{0:T(1024)S(1)} %broadcast_clamp_fusion.2), kind=kCustom, calls=%fused_computation.clone.clone.1 | custom fusion | bytes 4730880 | tf_op jit(solution)/shard_map/while/body/eval_jaxpr/jit(_take)/gather | solution.py:57
  388.3 5.1 convolution_add_fusion.2
  396.0 13.0 %gather_fusion = bf16[3072,384]{1,0:T(8,128)(2,1)} fusion(bf16[3584,384]{1,0:T(8,128)(2,1)S(1)} %get-tuple-element.187, s32[3072]{0:T(1024)S(1)} %broadcast_clamp_fusion.2), kind=kCustom, calls=%fused_computation.clone.clone.1 | custom fusion | bytes 4730880 | tf_op jit(solution)/shard_map/while/body/eval_jaxpr/jit(_take)/gather | solution.py:57
  409.0 5.1 convolution_add_fusion.2
  416.7 13.0 %gather_fusion = bf16[3072,384]{1,0:T(8,128)(2,1)} fusion(bf16[3584,384]{1,0:T(8,128)(2,1)S(1)} %get-tuple-element.187, s32[3072]{0:T(1024)S(1)} %broadcast_clamp_fusion.2), kind=kCustom, calls=%fused_computation.clone.clone.1 | custom fusion | bytes 4730880 | tf_op jit(solution)/shard_map/while/body/eval_jaxpr/jit(_take)/gather | solution.py:57
  429.8 5.1 convolution_add_fusion.2
  437.5 13.0 %gather_fusion = bf16[3072,384]{1,0:T(8,128)(2,1)} fusion(bf16[3584,384]{1,0:T(8,128)(2,1)S(1)} %get-tuple-element.187, s32[3072]{0:T(1024)S(1)} %broadcast_clamp_fusion.2), kind=kCustom, calls=%fused_computation.clone.clone.1 | custom fusion | bytes 4730880 | tf_op jit(solution)/shard_map/while/body/eval_jaxpr/jit(_take)/gather | solution.py:57
  450.5 5.1 convolution_add_fusion.2
  458.2 13.0 %gather_fusion = bf16[3072,384]{1,0:T(8,128)(2,1)} fusion(bf16[3584,384]{1,0:T(8,128)(2,1)S(1)} %get-tuple-element.187, s32[3072]{0:T(1024)S(1)} %broadcast_clamp_fusion.2), kind=kCustom, calls=%fused_computation.clone.clone.1 | custom fusion | bytes 4730880 | tf_op jit(solution)/shard_map/while/body/eval_jaxpr/jit(_take)/gather | solution.py:57
  471.3 5.1 convolution_add_fusion.2
  479.0 13.0 %gather_fusion = bf16[3072,384]{1,0:T(8,128)(2,1)} fusion(bf16[3584,384]{1,0:T(8,128)(2,1)S(1)} %get-tuple-element.187, s32[3072]{0:T(1024)S(1)} %broadcast_clamp_fusion.2), kind=kCustom, calls=%fused_computation.clone.clone.1 | custom fusion | bytes 4730880 | tf_op jit(solution)/shard_map/while/body/eval_jaxpr/jit(_take)/gather | solution.py:57
  492.0 5.1 convolution_add_fusion.2
  499.7 13.0 %gather_fusion = bf16[3072,384]{1,0:T(8,128)(2,1)} fusion(bf16[3584,384]{1,0:T(8,128)(2,1)S(1)} %get-tuple-element.187, s32[3072]{0:T(1024)S(1)} %broadcast_clamp_fusion.2), kind=kCustom, calls=%fused_computation.clone.clone.1 | custom fusion | bytes 4730880 | tf_op jit(solution)/shard_map/while/body/eval_jaxpr/jit(_take)/gather | solution.py:57
  512.8 5.1 convolution_add_fusion.2
  520.5 13.0 %gather_fusion = bf16[3072,384]{1,0:T(8,128)(2,1)} fusion(bf16[3584,384]{1,0:T(8,128)(2,1)S(1)} %get-tuple-element.187, s32[3072]{0:T(1024)S(1)} %broadcast_clamp_fusion.2), kind=kCustom, calls=%fused_computation.clone.clone.1 | custom fusion | bytes 4730880 | tf_op jit(solution)/shard_map/while/body/eval_jaxpr/jit(_take)/gather | solution.py:57
  533.5 5.1 convolution_add_fusion.2
  541.2 13.0 %gather_fusion = bf16[3072,384]{1,0:T(8,128)(2,1)} fusion(bf16[3584,384]{1,0:T(8,128)(2,1)S(1)} %get-tuple-element.187, s32[3072]{0:T(1024)S(1)} %broadcast_clamp_fusion.2), kind=kCustom, calls=%fused_computation.clone.clone.1 | custom fusion | bytes 4730880 | tf_op jit(solution)/shard_map/while/body/eval_jaxpr/jit(_take)/gather | solution.py:57
  554.3 5.1 convolution_add_fusion.2
  562.0 13.0 %gather_fusion = bf16[3072,384]{1,0:T(8,128)(2,1)} fusion(bf16[3584,384]{1,0:T(8,128)(2,1)S(1)} %get-tuple-element.187, s32[3072]{0:T(1024)S(1)} %broadcast_clamp_fusion.2), kind=kCustom, calls=%fused_computation.clone.clone.1 | custom fusion | bytes 4730880 | tf_op jit(solution)/shard_map/while/body/eval_jaxpr/jit(_take)/gather | solution.py:57
  582.7 13.0 %gather_fusion = bf16[3072,384]{1,0:T(8,128)(2,1)} fusion(bf16[3584,384]{1,0:T(8,128)(2,1)S(1)} %get-tuple-element.187, s32[3072]{0:T(1024)S(1)} %broadcast_clamp_fusion.2), kind=kCustom, calls=%fused_computation.clone.clone.1 | custom fusion | bytes 4730880 | tf_op jit(solution)/shard_map/while/body/eval_jaxpr/jit(_take)/gather | solution.py:57
  595.8 5.1 convolution_add_fusion.2
  603.5 13.0 %gather_fusion = bf16[3072,384]{1,0:T(8,128)(2,1)} fusion(bf16[3584,384]{1,0:T(8,128)(2,1)S(1)} %get-tuple-element.187, s32[3072]{0:T(1024)S(1)} %broadcast_clamp_fusion.2), kind=kCustom, calls=%fused_computation.clone.clone.1 | custom fusion | bytes 4730880 | tf_op jit(solution)/shard_map/while/body/eval_jaxpr/jit(_take)/gather | solution.py:57
  616.5 5.1 convolution_add_fusion.2
  624.2 13.0 %gather_fusion = bf16[3072,384]{1,0:T(8,128)(2,1)} fusion(bf16[3584,384]{1,0:T(8,128)(2,1)S(1)} %get-tuple-element.187, s32[3072]{0:T(1024)S(1)} %broadcast_clamp_fusion.2), kind=kCustom, calls=%fused_computation.clone.clone.1 | custom fusion | bytes 4730880 | tf_op jit(solution)/shard_map/while/body/eval_jaxpr/jit(_take)/gather | solution.py:57
  637.3 5.1 convolution_add_fusion.2
  645.0 13.0 %gather_fusion = bf16[3072,384]{1,0:T(8,128)(2,1)} fusion(bf16[3584,384]{1,0:T(8,128)(2,1)S(1)} %get-tuple-element.187, s32[3072]{0:T(1024)S(1)} %broadcast_clamp_fusion.2), kind=kCustom, calls=%fused_computation.clone.clone.1 | custom fusion | bytes 4730880 | tf_op jit(solution)/shard_map/while/body/eval_jaxpr/jit(_take)/gather | solution.py:57
  658.0 5.1 convolution_add_fusion.2
  664.8 158.6 %all-reduce.7.cloned.1.call-done = f32[27,192,384]{2,1,0:T(8,128)} async-done(((f32[27,192,384]{2,1,0:T(8,128)}), f32[27,192,384]{2,1,0:T(8,128)}) %all-reduce.7.cloned.1.call-update) | async-done | bytes 7962640 | tf_op jit(solution)/shard_map/psum | solution.py:13
  823.5 155.8 %all-reduce.9.cloned.1.call-done = f32[27,192,384]{2,1,0:T(8,128)} async-done(((f32[27,192,384]{2,1,0:T(8,128)}), f32[27,192,384]{2,1,0:T(8,128)}) %all-reduce.9.cloned.1.call-update) | async-done | bytes 7962640 | tf_op jit(solution)/shard_map/psum | solution.py:13
  982.2 153.1 %all-reduce.11.cloned.1.call-done = f32[27,192,384]{2,1,0:T(8,128)} async-done(((f32[27,192,384]{2,1,0:T(8,128)}), f32[27,192,384]{2,1,0:T(8,128)}) %all-reduce.11.cloned.1.call-update) | async-done | bytes 7962640 | tf_op jit(solution)/shard_map/psum | solution.py:13
  1135.3 7.4 copy.26
  (251 shorter events, 107.4 us)
Async XLA Ops:
  7.2 54.2 %copy-start.2 = (bf16[192,3072]{1,0:T(8,128)(2,1)S(1)}, bf16[192,3072]{1,0:T(8,128)(2,1)}, u32[]{:S(2)}) copy-start(bf16[192,3072]{1,0:T(8,128)(2,1)} %param.9) | copy-start | bytes 3538948
  7.2 53.5 %copy-start.4 = (f32[192]{0:T(256)S(1)}, f32[192]{0:T(256)}, u32[]{:S(2)}) copy-start(f32[192]{0:T(256)} %param.10) | copy-start | bytes 2308
  7.2 54.2 %copy-start.3 = (f32[192]{0:T(256)S(1)}, f32[192]{0:T(256)}, u32[]{:S(2)}) copy-start(f32[192]{0:T(256)} %param.11) | copy-start | bytes 2308
  7.2 79.1 %all-gather.2.cloned.1.call-start = ((), (), s32[]{:S(2)}) async-start(), calls=%async_computation | async-start | bytes 3538944 | tf_op jit(solution)/shard_map/all_gather | solution.py:49
  63.1 760.3 %all-reduce.7.cloned.1.call-start = ((), (), s32[]{:S(2)}) async-start(), calls=%async_computation.1 | async-start | bytes 15925248 | tf_op jit(solution)/shard_map/psum | solution.py:13
  87.4 7.2 collective-permute-start
  90.6 7.9 collective-permute-start.1
  119.2 4.4 copy-start
  119.2 4.4 copy-start.5
  139.3 5.1 copy-start
  139.3 5.1 copy-start.5
  160.0 5.1 copy-start
  160.0 5.1 copy-start.5
  180.8 5.1 copy-start
  180.8 5.1 copy-start.5
  201.5 5.1 copy-start
  201.5 5.1 copy-start.5
  222.3 5.1 copy-start
  222.3 5.1 copy-start.5
  243.0 5.1 copy-start
  243.0 5.1 copy-start.5
  263.8 5.1 copy-start
  263.8 5.1 copy-start.5
  284.5 5.1 copy-start
  284.5 5.1 copy-start.5
  305.3 5.1 copy-start
  305.3 5.1 copy-start.5
  326.0 5.1 copy-start
  326.0 5.1 copy-start.5
  346.8 5.1 copy-start
  346.8 5.1 copy-start.5
  367.5 5.1 copy-start
  367.5 5.1 copy-start.5
  388.3 5.1 copy-start
  388.3 5.1 copy-start.5
  409.0 5.1 copy-start
  409.0 5.1 copy-start.5
  429.8 5.1 copy-start
  429.8 5.1 copy-start.5
  450.5 5.1 copy-start
  450.5 5.1 copy-start.5
  471.3 5.1 copy-start
  471.3 5.1 copy-start.5
  492.0 5.1 copy-start
  492.0 5.1 copy-start.5
  512.8 5.1 copy-start
  512.8 5.1 copy-start.5
  533.5 5.1 copy-start
  533.5 5.1 copy-start.5
  554.3 5.1 copy-start
  554.3 5.1 copy-start.5
  575.0 5.1 copy-start
  575.0 5.1 copy-start.5
  595.8 5.1 copy-start
  595.8 5.1 copy-start.5
  616.5 5.1 copy-start
  616.5 5.1 copy-start.5
  637.3 5.1 copy-start
  637.3 5.1 copy-start.5
  658.0 5.1 copy-start
  658.0 5.1 copy-start.5
  664.8 314.5 %all-reduce.9.cloned.1.call-start = ((), (), s32[]{:S(2)}) async-start(), calls=%async_computation.2 | async-start | bytes 15925248 | tf_op jit(solution)/shard_map/psum | solution.py:13
  823.5 311.8 %all-reduce.11.cloned.1.call-start = ((), (), s32[]{:S(2)}) async-start(), calls=%async_computation.3 | async-start | bytes 15925248 | tf_op jit(solution)/shard_map/psum | solution.py:13
  979.3 1.7 copy-start.1
Sparse Core Ops, SparseCore 0:
  63.3 23.0 all-gather.1
  664.9 158.5 all-reduce.6
  826.0 153.3 all-reduce.8
  981.7 153.5 all-reduce.10
where the time goes:
time: 1150 us
  waiting for transfers between devices  497 us (43%)
  local copies, waits for them, and re-layouts  366 us (32%)
  matrix products  181 us (16%)
  blocking collectives  48.1 us (4%)
  other arithmetic  36.9 us (3%)
  between operations  14.6 us (1%)
    psum x3, waiting for transfers between devices, region_sum(): x = lax.psum(x, axis)  468 us
    gather x27, local copies, waits for them, and re-layouts, offset_step(): picked = jnp.take(gathered, position, axis=0, mode='fill', fill_value=0)  352 us
    dot_general x27, matrix products, offset_step(): lax.dot_general(kernel, picked, (((1,), (1,)), ((), ())), preferred_eleme...  137 us
    psum x6, blocking collectives, region_sum(): x = lax.psum(x, axis)  48.1 us
    dot_general x27, matrix products, offset_step(): grad_piece = jnp.dot(grad_out, picked, preferred_element_type=jnp.float32)  43.4 us
    select_n x27, other arithmetic, offset_step(): picked = jnp.take(gathered, position, axis=0, mode='fill', fill_value=0)  24.9 us
    all_gather x1, waiting for transfers between devices, per_device(): own_chans = lax.all_gather(site_rows, 'chan', axis=1, tiled=True)  23.1 us
  transfers between devices with their start and end apart: 6, of which 6 were waited for; matrix products, arithmetic and copies ran while one was open for 0% of the time, Pallas kernels for 0%

commit v1 on v0

--- a/solution.py
+++ b/solution.py
@@ -46,7 +46,9 @@
         * live_mask[None, :]
     )
     site_rows = jnp.transpose(normed).astype(jnp.bfloat16)
-    own_chans = lax.all_gather(site_rows, "chan", axis=1, tiled=True)
+    own_chans = jnp.concatenate(
+        lax.all_to_all(jnp.stack([site_rows] * lax.axis_size("chan")), "chan", 0, 0), axis=1
+    )
     gathered = padded(own_chans, border)
     anchor = region_idx * columns - border
     extent = columns + 2 * border

time: 1150 us -> 1140 us (level)
  waiting for transfers between devices: 497 us -> 473 us
  blocking collectives: 48.1 us -> 64.8 us
    all_gather x1 -> x0, waiting for transfers between devices: 23.1 us -> none  [per_device(): own_chans = lax.all_gather(site_rows, 'chan', axis=1, tiled=True)]
    all_to_all x0 -> x1, blocking collectives: none -> 16.7 us  [per_device(): lax.all_to_all(jnp.stack([site_rows] * lax.axis_size('chan')), 'chan', 0, 0)]
  transfers between devices with their start and end apart: 6 -> 5, of which waited for: 6 -> 5; matrix products, arithmetic and copies ran while one was open for 0% -> 0% of each run, Pallas kernels for 0% -> 0%
where the time goes in v1:
time: 1140 us
  waiting for transfers between devices  473 us (41%)
  local copies, waits for them, and re-layouts  365 us (32%)
  matrix products  181 us (16%)
  blocking collectives  64.8 us (6%)
  other arithmetic  34.4 us (3%)
  between operations  14.6 us (1%)
    psum x3, waiting for transfers between devices, region_sum(): x = lax.psum(x, axis)  466 us
    gather x27, local copies, waits for them, and re-layouts, offset_step(): picked = jnp.take(gathered, position, axis=0, mode='fill', fill_value=0)  352 us
    dot_general x27, matrix products, offset_step(): lax.dot_general(kernel, picked, (((1,), (1,)), ((), ())), preferred_eleme...  137 us
    psum x6, blocking collectives, region_sum(): x = lax.psum(x, axis)  48.1 us
    dot_general x27, matrix products, offset_step(): grad_piece = jnp.dot(grad_out, picked, preferred_element_type=jnp.float32)  43.4 us
    select_n x27, other arithmetic, offset_step(): picked = jnp.take(gathered, position, axis=0, mode='fill', fill_value=0)  24.9 us
  transfers between devices with their start and end apart: 5, of which 5 were waited for; matrix products, arithmetic and copies ran while one was open for 0% of the time, Pallas kernels for 0%

profile of v1, /device:TPU:1, one launch (start us, length us, event | category | flops | bytes accessed | tf_op | source)
XLA Modules:
  0.0 1138.2 jit_solution(3007058109829792364)
XLA Ops:
  10.2 9.9 all-reduce
  20.1 9.6 all-reduce.1
  29.7 10.4 all-reduce.2
  42.5 6.0 psum.90
  48.5 6.2 psum.91
  54.7 6.0 psum.92
  62.3 16.7 %all_to_all.5 = bf16[2,3072,192]{1,2,0:T(8,128)(2,1)S(1)} all-to-all(bf16[2,3072,192]{1,2,0:T(8,128)(2,1)S(1)} %pad_maximum_fusion.1), channel_id=1, replica_groups=mesh['z'=4,'y'=4,'x'=4,'chan'=2] {'chan'}, dimensions={0} | all-to-all | bytes 4718592 | tf_op jit(solution)/shard_map/all_to_all | solution.py:50
  95.5 559.6 %while.13 = (s32[]{:T(128)}, f32[192,3072]{1,0:T(8,128)}, f32[27,192,384]{2,1,0:T(8,128)}, bf16[27,192,384]{2,1,0:T(8,128)(2,1)}, s32[27,3072]{1,0:T(8,128)}, /*...) while((s32[]{:T(128)}, f32[192,3072]{1,0:T(8,128)}, ...), condition=%wide.region_13.14_spmd.clone, body=%wide.region_12.13_spmd.clone.sunk | while | flops 909548544 | bytes 30030000 | solution.py:67
  96.5 13.0 %gather_fusion = bf16[3072,384]{1,0:T(8,128)(2,1)} fusion(bf16[3584,384]{1,0:T(8,128)(2,1)S(1)} %get-tuple-element.187, s32[3072]{0:T(1024)S(1)} %broadcast_clamp_fusion.2), kind=kCustom, calls=%fused_computation.clone.clone.1 | custom fusion | bytes 4730880 | tf_op jit(solution)/shard_map/while/body/eval_jaxpr/jit(_take)/gather | solution.py:59
  116.5 13.0 %gather_fusion = bf16[3072,384]{1,0:T(8,128)(2,1)} fusion(bf16[3584,384]{1,0:T(8,128)(2,1)S(1)} %get-tuple-element.187, s32[3072]{0:T(1024)S(1)} %broadcast_clamp_fusion.2), kind=kCustom, calls=%fused_computation.clone.clone.1 | custom fusion | bytes 4730880 | tf_op jit(solution)/shard_map/while/body/eval_jaxpr/jit(_take)/gather | solution.py:59
  129.6 5.1 convolution_add_fusion.2
  137.3 13.0 %gather_fusion = bf16[3072,384]{1,0:T(8,128)(2,1)} fusion(bf16[3584,384]{1,0:T(8,128)(2,1)S(1)} %get-tuple-element.187, s32[3072]{0:T(1024)S(1)} %broadcast_clamp_fusion.2), kind=kCustom, calls=%fused_computation.clone.clone.1 | custom fusion | bytes 4730880 | tf_op jit(solution)/shard_map/while/body/eval_jaxpr/jit(_take)/gather | solution.py:59
  150.4 5.1 convolution_add_fusion.2
  158.0 13.0 %gather_fusion = bf16[3072,384]{1,0:T(8,128)(2,1)} fusion(bf16[3584,384]{1,0:T(8,128)(2,1)S(1)} %get-tuple-element.187, s32[3072]{0:T(1024)S(1)} %broadcast_clamp_fusion.2), kind=kCustom, calls=%fused_computation.clone.clone.1 | custom fusion | bytes 4730880 | tf_op jit(solution)/shard_map/while/body/eval_jaxpr/jit(_take)/gather | solution.py:59
  171.1 5.1 convolution_add_fusion.2
  178.8 13.0 %gather_fusion = bf16[3072,384]{1,0:T(8,128)(2,1)} fusion(bf16[3584,384]{1,0:T(8,128)(2,1)S(1)} %get-tuple-element.187, s32[3072]{0:T(1024)S(1)} %broadcast_clamp_fusion.2), kind=kCustom, calls=%fused_computation.clone.clone.1 | custom fusion | bytes 4730880 | tf_op jit(solution)/shard_map/while/body/eval_jaxpr/jit(_take)/gather | solution.py:59
  191.9 5.1 convolution_add_fusion.2
  199.5 13.0 %gather_fusion = bf16[3072,384]{1,0:T(8,128)(2,1)} fusion(bf16[3584,384]{1,0:T(8,128)(2,1)S(1)} %get-tuple-element.187, s32[3072]{0:T(1024)S(1)} %broadcast_clamp_fusion.2), kind=kCustom, calls=%fused_computation.clone.clone.1 | custom fusion | bytes 4730880 | tf_op jit(solution)/shard_map/while/body/eval_jaxpr/jit(_take)/gather | solution.py:59
  212.6 5.1 convolution_add_fusion.2
  220.3 13.0 %gather_fusion = bf16[3072,384]{1,0:T(8,128)(2,1)} fusion(bf16[3584,384]{1,0:T(8,128)(2,1)S(1)} %get-tuple-element.187, s32[3072]{0:T(1024)S(1)} %broadcast_clamp_fusion.2), kind=kCustom, calls=%fused_computation.clone.clone.1 | custom fusion | bytes 4730880 | tf_op jit(solution)/shard_map/while/body/eval_jaxpr/jit(_take)/gather | solution.py:59
  233.4 5.1 convolution_add_fusion.2
  241.0 13.0 %gather_fusion = bf16[3072,384]{1,0:T(8,128)(2,1)} fusion(bf16[3584,384]{1,0:T(8,128)(2,1)S(1)} %get-tuple-element.187, s32[3072]{0:T(1024)S(1)} %broadcast_clamp_fusion.2), kind=kCustom, calls=%fused_computation.clone.clone.1 | custom fusion | bytes 4730880 | tf_op jit(solution)/shard_map/while/body/eval_jaxpr/jit(_take)/gather | solution.py:59
  254.1 5.1 convolution_add_fusion.2
  261.8 13.0 %gather_fusion = bf16[3072,384]{1,0:T(8,128)(2,1)} fusion(bf16[3584,384]{1,0:T(8,128)(2,1)S(1)} %get-tuple-element.187, s32[3072]{0:T(1024)S(1)} %broadcast_clamp_fusion.2), kind=kCustom, calls=%fused_computation.clone.clone.1 | custom fusion | bytes 4730880 | tf_op jit(solution)/shard_map/while/body/eval_jaxpr/jit(_take)/gather | solution.py:59
  274.9 5.1 convolution_add_fusion.2
  282.5 13.0 %gather_fusion = bf16[3072,384]{1,0:T(8,128)(2,1)} fusion(bf16[3584,384]{1,0:T(8,128)(2,1)S(1)} %get-tuple-element.187, s32[3072]{0:T(1024)S(1)} %broadcast_clamp_fusion.2), kind=kCustom, calls=%fused_computation.clone.clone.1 | custom fusion | bytes 4730880 | tf_op jit(solution)/shard_map/while/body/eval_jaxpr/jit(_take)/gather | solution.py:59
  295.6 5.1 convolution_add_fusion.2
  303.3 13.0 %gather_fusion = bf16[3072,384]{1,0:T(8,128)(2,1)} fusion(bf16[3584,384]{1,0:T(8,128)(2,1)S(1)} %get-tuple-element.187, s32[3072]{0:T(1024)S(1)} %broadcast_clamp_fusion.2), kind=kCustom, calls=%fused_computation.clone.clone.1 | custom fusion | bytes 4730880 | tf_op jit(solution)/shard_map/while/body/eval_jaxpr/jit(_take)/gather | solution.py:59
  316.4 5.1 convolution_add_fusion.2
  324.0 13.0 %gather_fusion = bf16[3072,384]{1,0:T(8,128)(2,1)} fusion(bf16[3584,384]{1,0:T(8,128)(2,1)S(1)} %get-tuple-element.187, s32[3072]{0:T(1024)S(1)} %broadcast_clamp_fusion.2), kind=kCustom, calls=%fused_computation.clone.clone.1 | custom fusion | bytes 4730880 | tf_op jit(solution)/shard_map/while/body/eval_jaxpr/jit(_take)/gather | solution.py:59
  337.1 5.1 convolution_add_fusion.2
  344.8 13.0 %gather_fusion = bf16[3072,384]{1,0:T(8,128)(2,1)} fusion(bf16[3584,384]{1,0:T(8,128)(2,1)S(1)} %get-tuple-element.187, s32[3072]{0:T(1024)S(1)} %broadcast_clamp_fusion.2), kind=kCustom, calls=%fused_computation.clone.clone.1 | custom fusion | bytes 4730880 | tf_op jit(solution)/shard_map/while/body/eval_jaxpr/jit(_take)/gather | solution.py:59
  357.8 5.1 convolution_add_fusion.2
  365.5 13.0 %gather_fusion = bf16[3072,384]{1,0:T(8,128)(2,1)} fusion(bf16[3584,384]{1,0:T(8,128)(2,1)S(1)} %get-tuple-element.187, s32[3072]{0:T(1024)S(1)} %broadcast_clamp_fusion.2), kind=kCustom, calls=%fused_computation.clone.clone.1 | custom fusion | bytes 4730880 | tf_op jit(solution)/shard_map/while/body/eval_jaxpr/jit(_take)/gather | solution.py:59
  378.6 5.1 convolution_add_fusion.2
  386.3 13.0 %gather_fusion = bf16[3072,384]{1,0:T(8,128)(2,1)} fusion(bf16[3584,384]{1,0:T(8,128)(2,1)S(1)} %get-tuple-element.187, s32[3072]{0:T(1024)S(1)} %broadcast_clamp_fusion.2), kind=kCustom, calls=%fused_computation.clone.clone.1 | custom fusion | bytes 4730880 | tf_op jit(solution)/shard_map/while/body/eval_jaxpr/jit(_take)/gather | solution.py:59
  399.3 5.1 convolution_add_fusion.2
  407.0 13.0 %gather_fusion = bf16[3072,384]{1,0:T(8,128)(2,1)} fusion(bf16[3584,384]{1,0:T(8,128)(2,1)S(1)} %get-tuple-element.187, s32[3072]{0:T(1024)S(1)} %broadcast_clamp_fusion.2), kind=kCustom, calls=%fused_computation.clone.clone.1 | custom fusion | bytes 4730880 | tf_op jit(solution)/shard_map/while/body/eval_jaxpr/jit(_take)/gather | solution.py:59
  420.1 5.1 convolution_add_fusion.2
  427.8 13.0 %gather_fusion = bf16[3072,384]{1,0:T(8,128)(2,1)} fusion(bf16[3584,384]{1,0:T(8,128)(2,1)S(1)} %get-tuple-element.187, s32[3072]{0:T(1024)S(1)} %broadcast_clamp_fusion.2), kind=kCustom, calls=%fused_computation.clone.clone.1 | custom fusion | bytes 4730880 | tf_op jit(solution)/shard_map/while/body/eval_jaxpr/jit(_take)/gather | solution.py:59
  440.8 5.1 convolution_add_fusion.2
  448.5 13.0 %gather_fusion = bf16[3072,384]{1,0:T(8,128)(2,1)} fusion(bf16[3584,384]{1,0:T(8,128)(2,1)S(1)} %get-tuple-element.187, s32[3072]{0:T(1024)S(1)} %broadcast_clamp_fusion.2), kind=kCustom, calls=%fused_computation.clone.clone.1 | custom fusion | bytes 4730880 | tf_op jit(solution)/shard_map/while/body/eval_jaxpr/jit(_take)/gather | solution.py:59
  461.6 5.1 convolution_add_fusion.2
  469.3 13.0 %gather_fusion = bf16[3072,384]{1,0:T(8,128)(2,1)} fusion(bf16[3584,384]{1,0:T(8,128)(2,1)S(1)} %get-tuple-element.187, s32[3072]{0:T(1024)S(1)} %broadcast_clamp_fusion.2), kind=kCustom, calls=%fused_computation.clone.clone.1 | custom fusion | bytes 4730880 | tf_op jit(solution)/shard_map/while/body/eval_jaxpr/jit(_take)/gather | solution.py:59
  482.3 5.1 convolution_add_fusion.2
  490.0 13.0 %gather_fusion = bf16[3072,384]{1,0:T(8,128)(2,1)} fusion(bf16[3584,384]{1,0:T(8,128)(2,1)S(1)} %get-tuple-element.187, s32[3072]{0:T(1024)S(1)} %broadcast_clamp_fusion.2), kind=kCustom, calls=%fused_computation.clone.clone.1 | custom fusion | bytes 4730880 | tf_op jit(solution)/shard_map/while/body/eval_jaxpr/jit(_take)/gather | solution.py:59
  503.1 5.1 convolution_add_fusion.2
  510.8 13.0 %gather_fusion = bf16[3072,384]{1,0:T(8,128)(2,1)} fusion(bf16[3584,384]{1,0:T(8,128)(2,1)S(1)} %get-tuple-element.187, s32[3072]{0:T(1024)S(1)} %broadcast_clamp_fusion.2), kind=kCustom, calls=%fused_computation.clone.clone.1 | custom fusion | bytes 4730880 | tf_op jit(solution)/shard_map/while/body/eval_jaxpr/jit(_take)/gather | solution.py:59
  531.5 13.0 %gather_fusion = bf16[3072,384]{1,0:T(8,128)(2,1)} fusion(bf16[3584,384]{1,0:T(8,128)(2,1)S(1)} %get-tuple-element.187, s32[3072]{0:T(1024)S(1)} %broadcast_clamp_fusion.2), kind=kCustom, calls=%fused_computation.clone.clone.1 | custom fusion | bytes 4730880 | tf_op jit(solution)/shard_map/while/body/eval_jaxpr/jit(_take)/gather | solution.py:59
  544.6 5.1 convolution_add_fusion.2
  552.3 13.0 %gather_fusion = bf16[3072,384]{1,0:T(8,128)(2,1)} fusion(bf16[3584,384]{1,0:T(8,128)(2,1)S(1)} %get-tuple-element.187, s32[3072]{0:T(1024)S(1)} %broadcast_clamp_fusion.2), kind=kCustom, calls=%fused_computation.clone.clone.1 | custom fusion | bytes 4730880 | tf_op jit(solution)/shard_map/while/body/eval_jaxpr/jit(_take)/gather | solution.py:59
  565.3 5.1 convolution_add_fusion.2
  573.0 13.0 %gather_fusion = bf16[3072,384]{1,0:T(8,128)(2,1)} fusion(bf16[3584,384]{1,0:T(8,128)(2,1)S(1)} %get-tuple-element.187, s32[3072]{0:T(1024)S(1)} %broadcast_clamp_fusion.2), kind=kCustom, calls=%fused_computation.clone.clone.1 | custom fusion | bytes 4730880 | tf_op jit(solution)/shard_map/while/body/eval_jaxpr/jit(_take)/gather | solution.py:59
  586.1 5.1 convolution_add_fusion.2
  593.8 13.0 %gather_fusion = bf16[3072,384]{1,0:T(8,128)(2,1)} fusion(bf16[3584,384]{1,0:T(8,128)(2,1)S(1)} %get-tuple-element.187, s32[3072]{0:T(1024)S(1)} %broadcast_clamp_fusion.2), kind=kCustom, calls=%fused_computation.clone.clone.1 | custom fusion | bytes 4730880 | tf_op jit(solution)/shard_map/while/body/eval_jaxpr/jit(_take)/gather | solution.py:59
  606.8 5.1 convolution_add_fusion.2
  614.5 13.0 %gather_fusion = bf16[3072,384]{1,0:T(8,128)(2,1)} fusion(bf16[3584,384]{1,0:T(8,128)(2,1)S(1)} %get-tuple-element.187, s32[3072]{0:T(1024)S(1)} %broadcast_clamp_fusion.2), kind=kCustom, calls=%fused_computation.clone.clone.1 | custom fusion | bytes 4730880 | tf_op jit(solution)/shard_map/while/body/eval_jaxpr/jit(_take)/gather | solution.py:59
  627.6 5.1 convolution_add_fusion.2
  635.3 13.0 %gather_fusion = bf16[3072,384]{1,0:T(8,128)(2,1)} fusion(bf16[3584,384]{1,0:T(8,128)(2,1)S(1)} %get-tuple-element.187, s32[3072]{0:T(1024)S(1)} %broadcast_clamp_fusion.2), kind=kCustom, calls=%fused_computation.clone.clone.1 | custom fusion | bytes 4730880 | tf_op jit(solution)/shard_map/while/body/eval_jaxpr/jit(_take)/gather | solution.py:59
  648.3 5.1 convolution_add_fusion.2
  655.1 157.3 %all-reduce.7.cloned.1.call-done = f32[27,192,384]{2,1,0:T(8,128)} async-done(((f32[27,192,384]{2,1,0:T(8,128)}), f32[27,192,384]{2,1,0:T(8,128)}) %all-reduce.7.cloned.1.call-update) | async-done | bytes 7962640 | tf_op jit(solution)/shard_map/psum | solution.py:13
  812.5 155.8 %all-reduce.9.cloned.1.call-done = f32[27,192,384]{2,1,0:T(8,128)} async-done(((f32[27,192,384]{2,1,0:T(8,128)}), f32[27,192,384]{2,1,0:T(8,128)}) %all-reduce.9.cloned.1.call-update) | async-done | bytes 7962640 | tf_op jit(solution)/shard_map/psum | solution.py:13
  971.1 153.2 %all-reduce.11.cloned.1.call-done = f32[27,192,384]{2,1,0:T(8,128)} async-done(((f32[27,192,384]{2,1,0:T(8,128)}), f32[27,192,384]{2,1,0:T(8,128)}) %all-reduce.11.cloned.1.call-update) | async-done | bytes 7962640 | tf_op jit(solution)/shard_map/psum | solution.py:13
  1124.4 7.4 copy.27
  (250 shorter events, 104.1 us)
Async XLA Ops:
  7.2 54.2 %copy-start.2 = (bf16[192,3072]{1,0:T(8,128)(2,1)S(1)}, bf16[192,3072]{1,0:T(8,128)(2,1)}, u32[]{:S(2)}) copy-start(bf16[192,3072]{1,0:T(8,128)(2,1)} %param.9) | copy-start | bytes 3538948
  7.2 53.5 %copy-start.4 = (f32[192]{0:T(256)S(1)}, f32[192]{0:T(256)}, u32[]{:S(2)}) copy-start(f32[192]{0:T(256)} %param.10) | copy-start | bytes 2308
  7.2 54.2 %copy-start.3 = (f32[192]{0:T(256)S(1)}, f32[192]{0:T(256)}, u32[]{:S(2)}) copy-start(f32[192]{0:T(256)} %param.11) | copy-start | bytes 2308
  7.2 805.2 %all-reduce.7.cloned.1.call-start = ((), (), s32[]{:S(2)}) async-start(), calls=%async_computation.1 | async-start | bytes 15925248 | tf_op jit(solution)/shard_map/psum | solution.py:13
  79.1 7.5 collective-permute-start
  82.7 7.7 collective-permute-start.1
  109.5 4.4 copy-start
  109.5 4.4 copy-start.5
  129.6 5.1 copy-start
  129.6 5.1 copy-start.5
  150.3 5.1 copy-start
  150.3 5.1 copy-start.5
  171.1 5.1 copy-start
  171.1 5.1 copy-start.5
  191.8 5.1 copy-start
  191.8 5.1 copy-start.5
  212.6 5.1 copy-start
  212.6 5.1 copy-start.5
  233.3 5.1 copy-start
  233.3 5.1 copy-start.5
  254.1 5.1 copy-start
  254.1 5.1 copy-start.5
  274.8 5.1 copy-start
  274.8 5.1 copy-start.5
  295.6 5.1 copy-start
  295.6 5.1 copy-start.5
  316.3 5.1 copy-start
  316.3 5.1 copy-start.5
  337.1 5.1 copy-start
  337.1 5.1 copy-start.5
  357.8 5.1 copy-start
  357.8 5.1 copy-start.5
  378.6 5.1 copy-start
  378.6 5.1 copy-start.5
  399.3 5.1 copy-start
  399.3 5.1 copy-start.5
  420.1 5.1 copy-start
  420.1 5.1 copy-start.5
  440.8 5.1 copy-start
  440.8 5.1 copy-start.5
  461.6 5.1 copy-start
  461.6 5.1 copy-start.5
  482.3 5.1 copy-start
  482.3 5.1 copy-start.5
  503.1 5.1 copy-start
  503.1 5.1 copy-start.5
  523.8 5.1 copy-start
  523.8 5.1 copy-start.5
  544.6 5.1 copy-start
  544.6 5.1 copy-start.5
  565.3 5.1 copy-start
  565.3 5.1 copy-start.5
  586.1 5.1 copy-start
  586.1 5.1 copy-start.5
  606.8 5.1 copy-start
  606.8 5.1 copy-start.5
  627.6 5.1 copy-start
  627.6 5.1 copy-start.5
  648.3 5.1 copy-start
  648.3 5.1 copy-start.5
  655.1 313.2 %all-reduce.9.cloned.1.call-start = ((), (), s32[]{:S(2)}) async-start(), calls=%async_computation.2 | async-start | bytes 15925248 | tf_op jit(solution)/shard_map/psum | solution.py:13
  812.5 311.9 %all-reduce.11.cloned.1.call-start = ((), (), s32[]{:S(2)}) async-start(), calls=%async_computation.3 | async-start | bytes 15925248 | tf_op jit(solution)/shard_map/psum | solution.py:13
  968.3 1.7 copy-start.1
Sparse Core Ops, SparseCore 0:
  655.2 157.1 all-reduce.6
  814.9 153.3 all-reduce.8
  970.8 153.5 all-reduce.10
